TPU v7x, 512 devices: a whole 4x8x8 slice. The times are simulated.
512 devices in a mesh: tok: 64 (over x, z, core), mlp: 8 (over y).
Axes of the slice: x: 4, y: 8, z: 8, core: 2. Of those that a mesh axis runs over, the one named last changes fastest.
Arguments:
- queries: bfloat16 [4096, 7168], P('tok', 'mlp')
- fresh_token_keys: bfloat16 [4096, 1024], P('tok', 'mlp'), may hold values from -6 to 6
- fresh_token_values: bfloat16 [4096, 1024], P('tok', 'mlp'), may hold values from -6 to 6
- leaf_key_block: bfloat16 [20480, 1024], P('tok', 'mlp'), may hold values from -6 to 6
- leaf_value_block: bfloat16 [20480, 1024], P('tok', 'mlp'), may hold values from -6 to 6
- shared_key_block: bfloat16 [16384, 1024], P('tok', 'mlp'), may hold values from -6 to 6
- shared_value_block: bfloat16 [16384, 1024], P('tok', 'mlp'), may hold values from -6 to 6
- out_weight: bfloat16 [7168, 7168], P('mlp', 'tok'), may hold values from -0.0625 to 0.0625
- residual: bfloat16 [4096, 7168], P('mlp', 'tok'), may hold values from -2.5 to 2.5
- token_request: int32 [4096], replicated, may hold values from 0 to 63, as said below
- positions: int32 [4096], P('tok'), may hold values from 129 to 831, as said below
- parents: int32 [74], replicated, may hold values from -1 to 9, as said below
- node_lengths: int32 [74], replicated, may hold values from 1 to 256, as said below
- node_owner: int32 [74], replicated, may hold values from 0 to 63, as said below
Outputs:
- hidden: bfloat16 [4096, 7168], P('mlp', 'tok')
- leaf_key_output: bfloat16 [20480, 1024], P('tok', 'mlp')
- leaf_value_output: bfloat16 [20480, 1024], P('tok', 'mlp')
Inputs may be any that keep to these rules, and one draw needn't show every extreme that they name: `token_request`: index d of tok holds the 64 new tokens of the request whose leaf it owns (node_owner of that leaf is d), in some order. positions = node_lengths of the token's root, middle and leaf plus the token's rank among its request's new tokens; the ranks of one request are 0 to 63, each once. `parents`: nodes 0 to 1 are roots (parent -1), the next 8 are middle nodes with a root as parent, the last 64 are the leaves of requests 0, 1, ... with a middle node as parent; every root and middle node has a child; the leaf of request 0 lies below root 0. `node_lengths`: roots and middle nodes hold 64 to 256 tokens, root 0 and the middle node above leaf 0 exactly 256; leaves hold 1 to 256, leaf 0 exactly 256. `node_owner`: the 10 roots and middle nodes have different owners; the leaves' owners are a permutation of the indices of tok; a node's cache starts at row 0 of its owner's block.
All inputs are finite; a program needn't handle non-finite values.
Results may differ from a plain program's by a relative error of at most 0.012.
Values may be sent and summed in bfloat16 or wider, within the bound.
No kernel may reach another device: no remote copies, remote signals or barrier semaphores. Data moves between devices by JAX's collectives and lax.ppermute only.
A program may use at most 64 MiB of HBM per device.

v0:
```python
import math
import jax
import jax.numpy as jnp
from jax import lax
from jax.sharding import PartitionSpec as P

HEAD_SIZE = 128
ROOTS = 2
MIDS = 8
THETA = 5000000.0
NEG = -1e30


def apply_rotary(values, position, heads):
    width = values.shape[1] // heads
    half = width // 2
    table = values.astype(jnp.float32).reshape(values.shape[0], heads, width)
    freq = THETA ** (-(jnp.arange(half, dtype=jnp.float32) * 2.0) / width)
    angle = position.astype(jnp.float32)[:, None] * freq[None, :]
    cosine = jnp.cos(angle)[:, None, :]
    sine = jnp.sin(angle)[:, None, :]
    first = table[:, :, :half]
    second = table[:, :, half:]
    turned = jnp.concatenate(
        [first * cosine - second * sine, second * cosine + first * sine], axis=2
    )
    return turned.reshape(values.shape).astype(jnp.bfloat16)


def attend_key_block(queries4, keys, values, valid):
    scale = 1.0 / math.sqrt(queries4.shape[-1])
    scores = (
        jnp.einsum("sgqd,rgd->sgqr", queries4, keys, preferred_element_type=jnp.float32) * scale
    )
    allowed = valid[:, None, None, :]
    highest = jnp.max(jnp.where(allowed, scores, NEG), axis=3)
    weights = jnp.where(allowed, jnp.exp(scores - highest[..., None]), 0.0).astype(jnp.bfloat16)
    total = jnp.sum(weights.astype(jnp.float32), axis=3)
    output = jnp.einsum("sgqr,rgd->sgqd", weights, values, preferred_element_type=jnp.float32)
    return (highest, total, output)


def merge_state(state, block):
    high_a, total_a, out_a = state
    running_peak_b, running_sum_b, partial_output_b = block
    highest = jnp.maximum(high_a, running_peak_b)
    scale_a = jnp.exp(high_a - highest)
    scale_b = jnp.exp(running_peak_b - highest)
    return (
        highest,
        scale_a * total_a + scale_b * running_sum_b,
        scale_a[..., None] * out_a + scale_b[..., None] * partial_output_b,
    )


def lookup(table, index):
    return jnp.sum(jnp.where(jnp.arange(table.shape[0]) == index, table, 0))


def body(
    queries,
    fresh_token_keys,
    fresh_token_values,
    leaf_key_block,
    leaf_value_block,
    shared_key_block,
    shared_value_block,
    out_weight,
    residual,
    token_request,
    positions,
    parents,
    node_lengths,
    node_owner,
):
    my_index = lax.axis_index("tok")
    tok_rows = queries.shape[0]
    width = HEAD_SIZE
    q_heads = queries.shape[1] // width
    kv_heads = fresh_token_keys.shape[1] // width
    group = q_heads // kv_heads
    kv_width = kv_heads * width
    shared_count = ROOTS + MIDS
    query_turned = apply_rotary(queries, positions, q_heads)
    key_turned = apply_rotary(fresh_token_keys, positions, kv_heads)
    my_request = lax.dynamic_slice_in_dim(token_request, my_index * tok_rows, 1)[0]
    leaf_node = shared_count + my_request
    middle = lookup(parents, leaf_node)
    root = lookup(parents, middle)
    leaf_length = lookup(node_lengths, leaf_node)
    root_length = lookup(node_lengths, root)
    middle_length = lookup(node_lengths, middle)
    new_index = positions - root_length - middle_length - leaf_length
    leaf_rows = leaf_key_block.shape[0]
    row_ids = jnp.arange(leaf_rows)
    place = (row_ids[:, None] == (leaf_length + new_index)[None, :]).astype(jnp.bfloat16)
    pairs = jnp.concatenate([key_turned, fresh_token_values], axis=1)
    placed = jnp.dot(place, pairs, preferred_element_type=jnp.float32).astype(jnp.bfloat16)
    keep = row_ids[:, None] < leaf_length
    leaf_key_output = jnp.where(keep, leaf_key_block, placed[:, :kv_width])
    leaf_value_output = jnp.where(keep, leaf_value_block, placed[:, kv_width:])
    token_queries = query_turned.reshape(tok_rows, kv_heads, group, width)
    leaf_row_mask = row_ids[None, :] < (leaf_length + new_index + 1)[:, None]
    leaf_state = attend_key_block(
        token_queries,
        leaf_key_output.reshape(leaf_rows, kv_heads, width),
        leaf_value_output.reshape(leaf_rows, kv_heads, width),
        leaf_row_mask,
    )
    node_rows = shared_key_block.shape[0]
    root_owner = lookup(node_owner, root)
    middle_owner = lookup(node_owner, middle)
    gathered = (
        lax.all_gather(shared_key_block, "tok", axis=0, tiled=True),
        lax.all_gather(shared_value_block, "tok", axis=0, tiled=True),
    )
    root_keys = lax.dynamic_slice_in_dim(gathered[0], root_owner * node_rows, node_rows, 0)
    root_values = lax.dynamic_slice_in_dim(gathered[1], root_owner * node_rows, node_rows, 0)
    middle_keys = lax.dynamic_slice_in_dim(gathered[0], middle_owner * node_rows, node_rows, 0)
    middle_values = lax.dynamic_slice_in_dim(gathered[1], middle_owner * node_rows, node_rows, 0)
    node_ids = jnp.arange(node_rows)
    both_keys = jnp.concatenate([root_keys, middle_keys], axis=0).reshape(
        2 * node_rows, kv_heads, width
    )
    both_values = jnp.concatenate([root_values, middle_values], axis=0).reshape(
        2 * node_rows, kv_heads, width
    )
    both_valid = jnp.concatenate([node_ids < root_length, node_ids < middle_length], axis=0)
    shared_state = attend_key_block(token_queries, both_keys, both_values, both_valid[None, :])
    final = merge_state(shared_state, leaf_state)
    attended_local = (
        (final[2] / final[1][..., None]).reshape(tok_rows, q_heads * width).astype(jnp.bfloat16)
    )
    projected = jnp.dot(
        lax.all_gather(attended_local, "tok", axis=0, tiled=True),
        out_weight,
        preferred_element_type=jnp.float32,
    )
    summed = lax.psum_scatter(projected, "mlp", scatter_dimension=0, tiled=True)
    hidden = (residual.astype(jnp.float32) + summed).astype(jnp.bfloat16)
    return (hidden, leaf_key_output, leaf_value_output)


def solution(mesh):
    placed = (
        P("tok", "mlp"),
        P("tok", "mlp"),
        P("tok", "mlp"),
        P("tok", "mlp"),
        P("tok", "mlp"),
        P("tok", "mlp"),
        P("tok", "mlp"),
        P("mlp", "tok"),
        P("mlp", "tok"),
        P(),
        P("tok"),
        P(),
        P(),
        P(),
    )
    return jax.shard_map(
        body,
        mesh=mesh,
        in_specs=placed,
        out_specs=(P("mlp", "tok"), P("tok", "mlp"), P("tok", "mlp")),
        check_vma=False,
    )
```

profile of v0, /device:TPU:2, one launch (start us, length us, event | category | flops | bytes accessed | tf_op | source)
XLA Modules:
  0.0 330.6 jit_solution(14689822310884693069)
XLA Ops:
  7.2 0.7 all-gather.4.cloned.1.call-update
  8.0 0.7 all-gather.6.cloned.1.call-update
  8.7 1.3 dynamic_slice.15
  10.6 1.3 fusion.30
  11.9 1.9 select_reduce_fusion.4
  13.9 2.7 fusion.31
  17.7 1.0 reshape.252
  18.8 0.6 iota_compare_fusion.3
  19.4 0.6 iota_compare_fusion.5
  20.0 0.6 iota_compare_fusion.4
  20.6 1.9 broadcast_add_fusion
  22.5 0.7 bitcast_convert_fusion
  23.8 0.9 convolution_convert_fusion
  24.7 1.1 slice_select_fusion
  26.7 73.5 %all-gather.4.cloned.1.call-done = bf16[16384,128]{1,0:T(8,128)(2,1)} async-done(((bf16[256,128]{1,0:T(8,128)(2,1)}), bf16[16384,128]{1,0:T(8,128)(2,1)}) %all-gather.4.cloned.1.call-update) | async-done | bytes 4194320 | tf_op jit(solution)/shard_map/all_gather | solution.py:114
  100.2 0.9 constant_dynamic-slice_fusion.3
  101.1 0.4 select_reduce_fusion
  101.8 83.5 %all-gather.6.cloned.1.call-done = bf16[16384,128]{1,0:T(8,128)(2,1)} async-done(((bf16[256,128]{1,0:T(8,128)(2,1)}), bf16[16384,128]{1,0:T(8,128)(2,1)}) %all-gather.6.cloned.1.call-update) | async-done | bytes 4194320 | tf_op jit(solution)/shard_map/all_gather | solution.py:115
  185.4 0.9 constant_dynamic-slice_fusion.1
  187.0 0.7 copy.28
  187.8 86.2 %all-gather.8.cloned.1.call-done = bf16[4096,896]{1,0:T(8,128)(2,1)} async-done(((bf16[64,896]{1,0:T(8,128)(2,1)}), bf16[4096,896]{1,0:T(8,128)(2,1)}) %all-gather.8.cloned.1.call-update) | async-done | bytes 7340048 | tf_op jit(solution)/shard_map/all_gather | solution.py:135
  274.0 6.7 %fusion.43 = f32[4096,112]{0,1:T(8,128)} fusion(bf16[4096,896]{1,0:T(8,128)(2,1)} %all-gather.8.cloned.1.call-done, bf16[896,112]{0,1:T(8,128)(2,1)S(1)} %copy-done), kind=kOutput, calls=%fused_computation.91 | convolution fusion | flops 822083584 | bytes 9375744 | tf_op jit(solution)/shard_map/dot_general | solution.py:134
  280.7 41.7 %reduce-scatter.2.cloned.1.call-done = f32[512,112]{0,1:T(8,128)} async-done(((f32[4096,112]{0,1:T(8,128)}), f32[512,112]{0,1:T(8,128)}) %reduce-scatter.2.cloned.1.call-update) | async-done | bytes 229392 | tf_op jit(solution)/shard_map/reduce_scatter | solution.py:139
  322.4 1.6 add_convert_fusion
  (29 shorter events, 2.8 us)
Async XLA Ops:
  7.2 266.8 %copy-start = (bf16[896,112]{0,1:T(8,128)(2,1)S(1)}, bf16[896,112]{0,1:T(8,128)(2,1)}, u32[]{:S(2)}) copy-start(bf16[896,112]{0,1:T(8,128)(2,1)} %param.21) | copy-start | bytes 602116
  7.2 93.0 %all-gather.4.cloned.1.call-start = ((), (), s32[]{:S(2)}) async-start(), calls=%async_computation.1 | async-start | bytes 4259840 | tf_op jit(solution)/shard_map/all_gather | solution.py:114
  7.9 177.5 %all-gather.6.cloned.1.call-start = ((), (), s32[]{:S(2)}) async-start(), calls=%async_computation.2 | async-start | bytes 4259840 | tf_op jit(solution)/shard_map/all_gather | solution.py:115
  8.7 265.3 %all-gather.8.cloned.1.call-start = ((), (), s32[]{:S(2)}) async-start(), calls=%async_computation.3 | async-start | bytes 7454720 | tf_op jit(solution)/shard_map/all_gather | solution.py:135
  25.8 161.2 %copy-start.1 = (bf16[320,128]{1,0:T(8,128)(2,1)}, bf16[320,128]{1,0:T(8,128)(2,1)S(1)}, u32[]{:S(2)}) copy-start(bf16[320,128]{1,0:T(8,128)(2,1)S(1)} %get-tuple-element.22) | copy-start | bytes 245764
  25.8 161.2 %copy-start.3 = (bf16[320,128]{1,0:T(8,128)(2,1)}, bf16[320,128]{1,0:T(8,128)(2,1)S(1)}, u32[]{:S(2)}) copy-start(bf16[320,128]{1,0:T(8,128)(2,1)S(1)} %get-tuple-element.21) | copy-start | bytes 245764
  187.7 134.7 %copy-start.2 = (bf16[512,112]{0,1:T(8,128)(2,1)S(1)}, bf16[512,112]{0,1:T(8,128)(2,1)}, u32[]{:S(2)}) copy-start(bf16[512,112]{0,1:T(8,128)(2,1)} %param.22) | copy-start | bytes 344068
  187.7 134.7 %reduce-scatter.2.cloned.1.call-start = ((), (), s32[]{:S(2)}) async-start(), calls=%async_computation.4 | async-start | bytes 2064384 | tf_op jit(solution)/shard_map/reduce_scatter | solution.py:139
Sparse Core Ops, SparseCore 0:
  11.4 88.7 all-gather.3
  103.5 81.7 all-gather.5
  189.3 84.6 all-gather.7
  280.9 41.5 reduce-scatter.1
where the time goes:
time: 331 us
  waiting for transfers between devices  286 us (86%)
  between operations  15.8 us (5%)
  other arithmetic  14.3 us (4%)
  matrix products  9.1 us (3%)
  local copies, waits for them, and re-layouts  4.98 us (2%)
    all_gather x1, waiting for transfers between devices, body(): lax.all_gather(attended_local, 'tok', axis=0, tiled=True)  86.2 us
    all_gather x1, waiting for transfers between devices, body(): lax.all_gather(shared_value_block, 'tok', axis=0, tiled=True)  83.5 us
    all_gather x1, waiting for transfers between devices, body(): lax.all_gather(shared_key_block, 'tok', axis=0, tiled=True)  73.5 us
    reduce_scatter x1, waiting for transfers between devices, body(): summed = lax.psum_scatter(projected, 'mlp', scatter_dimension=0, tiled=True)  41.7 us
    dot_general x1, matrix products, body(): jnp.dot(lax.all_gather(attended_local, 'tok', axis=0, tiled=True), out_we...  6.74 us
  transfers between devices with their start and end apart: 4, of which 4 were waited for; matrix products, arithmetic and copies ran while one was open for 5% of the time, Pallas kernels for 0%

commit v1 on v0

--- a/solution.py
+++ b/solution.py
@@ -111,7 +111,10 @@
     root_owner = lookup(node_owner, root)
     middle_owner = lookup(node_owner, middle)
     gathered = (
-        lax.all_gather(shared_key_block, "tok", axis=0, tiled=True),
+        jnp.concatenate(
+            lax.all_to_all(jnp.stack([shared_key_block] * lax.axis_size("tok")), "tok", 0, 0),
+            axis=0,
+        ),
         lax.all_gather(shared_value_block, "tok", axis=0, tiled=True),
     )
     root_keys = lax.dynamic_slice_in_dim(gathered[0], root_owner * node_rows, node_rows, 0)

time: 331 us -> 279 us (0.84)
  waiting for transfers between devices: 286 us -> 222 us
  starting transfers between devices: 0.16 us -> 14.3 us
  other arithmetic: 14.3 us -> 10.3 us
    all_to_all x0 -> x1, waiting for transfers between devices: none -> 93.4 us  [body(): lax.all_to_all(jnp.stack([shared_key_block] * lax.axis_size('tok')), 'tok...]
    all_gather x1, waiting for transfers between devices: 83.5 us -> 0.02 us  [body(): lax.all_gather(shared_value_block, 'tok', axis=0, tiled=True)]
    all_gather x1 -> x0, waiting for transfers between devices: 73.5 us -> none  [body(): lax.all_gather(shared_key_block, 'tok', axis=0, tiled=True)]
    all_to_all x0 -> x1, starting transfers between devices: none -> 14.2 us  [body(): lax.all_to_all(jnp.stack([shared_key_block] * lax.axis_size('tok')), 'tok...]
    another operation x0 -> x1, local copies, waits for them, and re-layouts: none -> 3.86 us  [body(): jnp.stack([shared_key_block] * lax.axis_size('tok'))]
  transfers between devices with their start and end apart: 4 -> 4, of which waited for: 4 -> 3; matrix products, arithmetic and copies ran while one was open for 5% -> 4% of each run, Pallas kernels for 0% -> 0%
where the time goes in v1:
time: 279 us
  waiting for transfers between devices  222 us (80%)
  between operations  16 us (6%)
  starting transfers between devices  14.3 us (5%)
  other arithmetic  10.3 us (4%)
  matrix products  8.37 us (3%)
  local copies, waits for them, and re-layouts  8 us (3%)
    all_to_all x1, waiting for transfers between devices, body(): lax.all_to_all(jnp.stack([shared_key_block] * lax.axis_size('tok')), 'tok...  93.4 us
    all_gather x1, waiting for transfers between devices, body(): lax.all_gather(attended_local, 'tok', axis=0, tiled=True)  86 us
    reduce_scatter x1, waiting for transfers between devices, body(): summed = lax.psum_scatter(projected, 'mlp', scatter_dimension=0, tiled=True)  41.7 us
    all_to_all x1, starting transfers between devices, body(): lax.all_to_all(jnp.stack([shared_key_block] * lax.axis_size('tok')), 'tok...  14.2 us
    dot_general x1, matrix products, body(): jnp.dot(lax.all_gather(attended_local, 'tok', axis=0, tiled=True), out_we...  6.73 us
  transfers between devices with their start and end apart: 4, of which 3 were waited for; matrix products, arithmetic and copies ran while one was open for 4% of the time, Pallas kernels for 0%

profile of v1, /device:TPU:2, one launch (start us, length us, event | category | flops | bytes accessed | tf_op | source)
XLA Modules:
  0.0 278.8 jit_solution(16083135580632722029)
XLA Ops:
  7.2 3.9 %stack.2 = bf16[64,256,128]{2,1,0:T(8,128)(2,1)} broadcast(bf16[256,128]{1,0:T(8,128)(2,1)} %param.19), dimensions={1,2} | broadcast | bytes 4259840 | tf_op jit(solution)/shard_map/stack | solution.py:115
  11.1 14.2 %all-to-all-start = ((bf16[64,256,128]{2,1,0:T(8,128)(2,1)}), bf16[64,256,128]{2,1,0:T(8,128)(2,1)}, u32[]{:S(2)}, u32[]{:S(2)}) async-start(bf16[64,256,128]{2,1,0:T(8,128)(2,1)} %stack.2), calls=%async_computation | async-start | bytes 8388608 | tf_op jit(solution)/shard_map/all_to_all | solution.py:115
  25.4 0.7 all-gather.3.cloned.1.call-update
  26.1 1.3 dynamic_slice.15
  28.1 0.6 fusion.30
  28.7 1.3 select_reduce_fusion.4
  30.0 2.0 fusion.31
  33.5 0.7 iota_compare_fusion.4
  34.2 0.6 iota_compare_fusion.5
  34.8 0.7 iota_compare_fusion.3
  35.5 1.3 broadcast_add_fusion
  38.0 0.4 select_reduce_fusion.1
  38.7 93.4 %all-to-all-done = bf16[64,256,128]{2,1,0:T(8,128)(2,1)} async-done(((bf16[64,256,128]{2,1,0:T(8,128)(2,1)}), bf16[64,256,128]{2,1,0:T(8,128)(2,1)}, u32[]{:S(2)}, u32[]{:S(2)}) %all-to-all-start) | async-done | bytes 4194336 | tf_op jit(solution)/shard_map/all_to_all | solution.py:115
  132.1 0.9 constant_dynamic-slice_fusion.3
  133.0 0.4 select_reduce_fusion
  133.4 0.3 convert_reduce_fusion
  133.8 0.9 constant_dynamic-slice_fusion.1
  134.7 0.3 fusion.5
  135.0 0.3 fusion.7
  135.4 0.7 copy.28
  136.2 86.0 %all-gather.5.cloned.1.call-done = bf16[4096,896]{1,0:T(8,128)(2,1)} async-done(((bf16[64,896]{1,0:T(8,128)(2,1)}), bf16[4096,896]{1,0:T(8,128)(2,1)}) %all-gather.5.cloned.1.call-update) | async-done | bytes 7340048 | tf_op jit(solution)/shard_map/all_gather | solution.py:138
  222.2 6.7 %fusion.43 = f32[4096,112]{0,1:T(8,128)} fusion(bf16[4096,896]{1,0:T(8,128)(2,1)} %all-gather.5.cloned.1.call-done, bf16[896,112]{0,1:T(8,128)(2,1)S(1)} %copy-done), kind=kOutput, calls=%fused_computation.91 | convolution fusion | flops 822083584 | bytes 9375744 | tf_op jit(solution)/shard_map/dot_general | solution.py:137
  229.0 41.7 %reduce-scatter.2.cloned.1.call-done = f32[512,112]{0,1:T(8,128)} async-done(((f32[4096,112]{0,1:T(8,128)}), f32[512,112]{0,1:T(8,128)}) %reduce-scatter.2.cloned.1.call-update) | async-done | bytes 229392 | tf_op jit(solution)/shard_map/reduce_scatter | solution.py:142
  270.7 1.6 add_convert_fusion
  (47 shorter events, 1.9 us)
Async XLA Ops:
  7.2 215.1 %copy-start = (bf16[896,112]{0,1:T(8,128)(2,1)S(1)}, bf16[896,112]{0,1:T(8,128)(2,1)}, u32[]{:S(2)}) copy-start(bf16[896,112]{0,1:T(8,128)(2,1)} %param.21) | copy-start | bytes 602116
  11.0 17.0 %copy-start.12 = (s32[74]{0:T(128)S(1)}, s32[74]{0:T(128)}, u32[]{:S(2)}) copy-start(s32[74]{0:T(128)} %param.25) | copy-start | bytes 892
  11.0 18.9 %copy-start.9 = (s32[74]{0:T(128)S(1)}, s32[74]{0:T(128)}, u32[]{:S(2)}) copy-start(s32[74]{0:T(128)} %param.26) | copy-start | bytes 892
  11.0 18.9 %copy-start.10 = (s32[74]{0:T(128)S(1)}, s32[74]{0:T(128)}, u32[]{:S(2)}) copy-start(s32[74]{0:T(128)} %param.27) | copy-start | bytes 892
  11.1 22.2 %copy-start.3 = (bf16[64,896]{1,0:T(8,128)(2,1)S(1)}, bf16[64,896]{1,0:T(8,128)(2,1)}, u32[]{:S(2)}) copy-start(bf16[64,896]{1,0:T(8,128)(2,1)} %param.14) | copy-start | bytes 344068
  11.1 24.4 %copy-start.11 = (s32[64]{0:T(128)S(1)}, s32[64]{0:T(128)}, u32[]{:S(2)}) copy-start(s32[64]{0:T(128)} %param.24) | copy-start | bytes 772
  11.1 25.8 %copy-start.7 = (bf16[64,128]{1,0:T(8,128)(2,1)S(1)}, bf16[64,128]{1,0:T(8,128)(2,1)}, u32[]{:S(2)}) copy-start(bf16[64,128]{1,0:T(8,128)(2,1)} %param.15) | copy-start | bytes 49156
  11.1 26.3 %copy-start.8 = (bf16[64,128]{1,0:T(8,128)(2,1)S(1)}, bf16[64,128]{1,0:T(8,128)(2,1)}, u32[]{:S(2)}) copy-start(bf16[64,128]{1,0:T(8,128)(2,1)} %param.16) | copy-start | bytes 49156
  11.1 26.5 %copy-start.4 = (bf16[320,128]{1,0:T(8,128)(2,1)S(1)}, bf16[320,128]{1,0:T(8,128)(2,1)}, u32[]{:S(2)}) copy-start(bf16[320,128]{1,0:T(8,128)(2,1)} %param.18) | copy-start | bytes 245764
  11.1 26.5 %copy-start.5 = (bf16[320,128]{1,0:T(8,128)(2,1)S(1)}, bf16[320,128]{1,0:T(8,128)(2,1)}, u32[]{:S(2)}) copy-start(bf16[320,128]{1,0:T(8,128)(2,1)} %param.17) | copy-start | bytes 245764
  11.1 121.0 %all-to-all-start = ((bf16[64,256,128]{2,1,0:T(8,128)(2,1)}), bf16[64,256,128]{2,1,0:T(8,128)(2,1)}, u32[]{:S(2)}, u32[]{:S(2)}) async-start(bf16[64,256,128]{2,1,0:T(8,128)(2,1)} %stack.2), calls=%async_computation | async-start | bytes 8388608 | tf_op jit(solution)/shard_map/all_to_all | solution.py:115
  25.3 108.4 %all-gather.3.cloned.1.call-start = ((), (), s32[]{:S(2)}) async-start(), calls=%async_computation.2 | async-start | bytes 4259840 | tf_op jit(solution)/shard_map/all_gather | solution.py:118
  26.1 196.2 %all-gather.5.cloned.1.call-start = ((), (), s32[]{:S(2)}) async-start(), calls=%async_computation.3 | async-start | bytes 7454720 | tf_op jit(solution)/shard_map/all_gather | solution.py:138
  37.7 97.6 %copy-start.1 = (bf16[320,128]{1,0:T(8,128)(2,1)}, bf16[320,128]{1,0:T(8,128)(2,1)S(1)}, u32[]{:S(2)}) copy-start(bf16[320,128]{1,0:T(8,128)(2,1)S(1)} %get-tuple-element.22) | copy-start | bytes 245764
  37.7 97.6 %copy-start.6 = (bf16[320,128]{1,0:T(8,128)(2,1)}, bf16[320,128]{1,0:T(8,128)(2,1)S(1)}, u32[]{:S(2)}) copy-start(bf16[320,128]{1,0:T(8,128)(2,1)S(1)} %get-tuple-element.21) | copy-start | bytes 245764
  136.1 134.5 %copy-start.2 = (bf16[512,112]{0,1:T(8,128)(2,1)S(1)}, bf16[512,112]{0,1:T(8,128)(2,1)}, u32[]{:S(2)}) copy-start(bf16[512,112]{0,1:T(8,128)(2,1)} %param.22) | copy-start | bytes 344068
  136.1 134.5 %reduce-scatter.2.cloned.1.call-start = ((), (), s32[]{:S(2)}) async-start(), calls=%async_computation.4 | async-start | bytes 2064384 | tf_op jit(solution)/shard_map/reduce_scatter | solution.py:142
Sparse Core Ops, SparseCore 0:
  29.5 101.8 all-gather.2
  136.2 85.9 all-gather.4
  229.1 41.5 reduce-scatter.1
